TPU v7x, 512 devices: a whole 4x4x16 slice. The times are simulated.
512 devices in a mesh: phase: 16 (over x, z_hi), slab: 32 (over z_lo, y, core).
Axes of the slice: x: 4, y: 4, z: 16 (z_hi: 4, z_lo: 4; z = z_hi * 4 + z_lo), core: 2. Of those that a mesh axis runs over, the one named last changes fastest.
Arguments:
- pressure: float32 [2, 64, 32, 98304], P(None, 'phase', None, 'slab'), may hold values from -6 to 6
- mode_shapes: float32 [1024, 98304], P('phase', 'slab'), may hold values from -0.0390625 to 0.0390625
- point_weight: float32 [98304], P('slab'), may hold values from 0.5 to 2
- panel_order: int32 [8], replicated, may hold values from 0 to 7, each once
Outputs:
- influence: float32 [2, 64, 32, 1024], P(None, None, 'phase', 'slab')
Inputs may be any that keep to these rules, and one draw needn't show every extreme that they name: panel_order names each of 0 to 7 once.
All inputs are finite; a program needn't handle non-finite values.
Results may differ from a plain program's by a relative error of at most 0.00007.
Values sent between devices are 32-bit elements; how exact they have to be, the bound alone decides.
No kernel may reach another device: no remote copies, remote signals or barrier semaphores. Data moves between devices by JAX's collectives and lax.ppermute only.
A program may use at most 64 MiB of HBM per device.

v0:
```python
import math
import jax
import jax.numpy as jnp
from jax import lax
from jax.sharding import PartitionSpec as P


def blade_table(blades, count):
    phases = jnp.arange(count, dtype=jnp.int32)
    target = jnp.arange(blades, dtype=jnp.int32)
    index = target[:, None] * phases[None, :] % blades
    theta = index.astype(jnp.float32) * (2.0 * math.pi / blades)
    cosine = jnp.cos(theta)
    sine = jnp.sin(theta)
    upper = jnp.concatenate([cosine, -sine], axis=1)
    lower = jnp.concatenate([sine, cosine], axis=1)
    return jnp.concatenate([upper, lower], axis=0) * (1.0 / math.sqrt(blades))


def shards(pressure, mode_shapes, point_weight, panel_order):
    weighted = mode_shapes * point_weight[None, :]
    phase_dev = pressure.shape[1]
    excite = pressure.shape[2]
    rows = pressure.reshape(2 * phase_dev * excite, pressure.shape[3])
    partial_forces = lax.dot_general(
        rows,
        lax.all_gather(weighted, "phase", axis=0, tiled=True),
        (((1,), (1,)), ((), ())),
        precision=lax.Precision.HIGHEST,
        preferred_element_type=jnp.float32,
    )
    row_count = partial_forces.shape[0]
    panel_count = panel_order.shape[0]
    panels = partial_forces.reshape(row_count, panel_count, -1)
    selector = (panel_order[:, None] == jnp.arange(panel_count, dtype=jnp.int32)[None, :]).astype(
        jnp.float32
    )
    reordered = jnp.einsum(
        "rqc,pq->rpc", panels, selector, precision=lax.Precision.HIGHEST
    ).reshape(row_count, -1)
    share = lax.psum_scatter(reordered, "slab", scatter_dimension=1, tiled=True)
    mode_local = share.shape[1]
    forces = share.reshape(2, phase_dev, excite, mode_local)
    blades = phase_dev * lax.axis_size("phase")
    gathered = lax.all_to_all(forces, "phase", split_axis=2, concat_axis=1, tiled=True)
    table = blade_table(blades, blades)
    result = jnp.dot(
        table,
        gathered.reshape(2 * blades, -1),
        precision=lax.Precision.HIGHEST,
        preferred_element_type=jnp.float32,
    )
    result = result.reshape(2, blades, -1, mode_local)
    return result


def solution(mesh):
    placed = (P(None, "phase", None, "slab"), P("phase", "slab"), P("slab"), P())
    return jax.shard_map(
        shards,
        mesh=mesh,
        in_specs=placed,
        out_specs=P(None, None, "phase", "slab"),
        check_vma=False,
    )
```

profile of v0, /device:TPU:2, one launch (start us, length us, event | category | flops | bytes accessed | tf_op | source)
XLA Modules:
  0.0 522.7 jit_solution(7747216759934679100)
XLA Ops:
  6.5 0.0 copy-start
  6.5 0.0 copy-start.1
  6.5 0.0 all-gather.2.cloned.1.call-start
  6.5 2.3 broadcast_multiply_fusion
  8.8 0.0 all-gather.2.cloned.1.call-update
  8.8 0.0 reduce-scatter.4.cloned.1.call-start
  8.9 307.7 %all-gather.2.cloned.1.call-done = f32[1024,3072]{1,0:T(8,128)} async-done(((f32[64,3072]{1,0:T(8,128)}), f32[1024,3072]{1,0:T(8,128)}) %all-gather.2.cloned.1.call-update) | async-done | bytes 12582928 | tf_op jit(solution)/shard_map/all_gather | solution.py:27
  316.6 0.0 copy-done
  316.6 13.5 %fusion.12 = f32[1024,256]{1,0:T(8,128)} fusion(f32[1024,3072]{1,0:T(8,128)} %all-gather.2.cloned.1.call-done, f32[256,3072]{1,0:T(8,128)S(1)} %bitcast.35), kind=kOutput, calls=%fused_computation.19 | convolution fusion | flops 9663676416 | bytes 16777216 | tf_op jit(solution)/shard_map/dot_general | solution.py:25
  330.1 2.5 copy.12
  332.6 0.0 copy-done.1
  332.6 2.9 convolution_bitcast_fusion
  335.5 2.5 copy.20
  338.0 0.0 reduce-scatter.4.cloned.1.call-update
  338.1 0.1 fusion.6
  338.2 147.6 %reduce-scatter.4.cloned.1.call-done = f32[32,256]{1,0:T(8,128)} async-done(((f32[1024,256]{1,0:T(8,128)}), f32[32,256]{1,0:T(8,128)}) %reduce-scatter.4.cloned.1.call-update) | async-done | bytes 32784
  485.8 0.9 copy.19
  486.7 0.1 copy.22
  486.8 0.8 reshape.39
  487.5 12.2 %all-to-all-start = ((f32[16,1,512]{2,1,0:T(1,128)}), f32[16,1,512]{2,1,0:T(1,128)S(1)}, u32[]{:S(2)}, u32[]{:S(2)}) async-start(f32[16,1,512]{2,1,0:T(1,128)} %reshape.39), calls=%async_computation | async-start | bytes 65536 | tf_op jit(solution)/shard_map/all_to_all | solution.py:45
  499.8 0.1 fusion.8
  499.9 0.1 maximum_multiply_fusion
  500.0 13.2 %all-to-all-done = f32[16,1,512]{2,1,0:T(1,128)S(1)} async-done(((f32[16,1,512]{2,1,0:T(1,128)}), f32[16,1,512]{2,1,0:T(1,128)S(1)}, u32[]{:S(2)}, u32[]{:S(2)}) %all-to-all-start) | async-done | bytes 32800 | tf_op jit(solution)/shard_map/all_to_all | solution.py:45
  513.2 0.5 broadcast.24
  513.7 0.7 reduce
  514.4 0.1 reshape.40
  514.6 0.1 reshape.33
  514.8 0.1 copy.16
  514.8 1.0 fusion.13
  (2 shorter events, 0.1 us)
Async XLA Ops:
  6.5 310.1 %copy-start = (f32[2,4,32,3072]{3,2,1,0:T(8,128)S(1)}, f32[2,4,32,3072]{3,2,1,0:T(8,128)}, u32[]{:S(2)}) copy-start(f32[2,4,32,3072]{3,2,1,0:T(8,128)} %param.4) | copy-start | bytes 9437188
  6.5 326.1 %copy-start.1 = (s32[8]{0:T(128)S(1)}, s32[8]{0:T(128)}, u32[]{:S(2)}) copy-start(s32[8]{0:T(128)} %param.7) | copy-start | bytes 100
  6.5 310.1 %all-gather.2.cloned.1.call-start = ((), (), s32[]{:S(2)}) async-start(), calls=%async_computation.2 | async-start | bytes 13369344 | tf_op jit(solution)/shard_map/all_gather | solution.py:27
  8.8 477.0 %reduce-scatter.4.cloned.1.call-start = ((), (), s32[]{:S(2)}) async-start(), calls=%async_computation.3 | async-start | bytes 1081344
  487.5 25.7 %all-to-all-start = ((f32[16,1,512]{2,1,0:T(1,128)}), f32[16,1,512]{2,1,0:T(1,128)S(1)}, u32[]{:S(2)}, u32[]{:S(2)}) async-start(f32[16,1,512]{2,1,0:T(1,128)} %reshape.39), calls=%async_computation | async-start | bytes 65536 | tf_op jit(solution)/shard_map/all_to_all | solution.py:45
Sparse Core Ops, SparseCore 0:
  10.4 306.1 all-gather.1
  338.2 147.6 reduce-scatter.3
where the time goes:
time: 523 us
  waiting for transfers between devices  469 us (90%)
  matrix products  17.3 us (3%)
  between operations  13.5 us (3%)
  starting transfers between devices  12.2 us (2%)
  local copies, waits for them, and re-layouts  7.67 us (1%)
    all_gather x1, waiting for transfers between devices, shards(): lax.all_gather(weighted, 'phase', axis=0, tiled=True)  308 us
    unnamed x3, waiting for transfers between devices  148 us
    dot_general x1, matrix products, shards(): lax.dot_general(rows, lax.all_gather(weighted, 'phase', axis=0, tiled=Tru...  13.5 us
    all_to_all x1, waiting for transfers between devices, shards(): lax.all_to_all(forces, 'phase', split_axis=2, concat_axis=1, tiled=True)  13.2 us
    all_to_all x1, starting transfers between devices, shards(): lax.all_to_all(forces, 'phase', split_axis=2, concat_axis=1, tiled=True)  12.2 us
  transfers between devices with their start and end apart: 3, of which 3 were waited for; matrix products, arithmetic and copies ran while one was open for 0% of the time, Pallas kernels for 0%

commit v1 on v0

--- a/solution.py
+++ b/solution.py
@@ -24,7 +24,9 @@
     rows = pressure.reshape(2 * phase_dev * excite, pressure.shape[3])
     partial_forces = lax.dot_general(
         rows,
-        lax.all_gather(weighted, "phase", axis=0, tiled=True),
+        jnp.concatenate(
+            lax.all_to_all(jnp.stack([weighted] * lax.axis_size("phase")), "phase", 0, 0), axis=0
+        ),
         (((1,), (1,)), ((), ())),
         precision=lax.Precision.HIGHEST,
         preferred_element_type=jnp.float32,

time: 523 us -> 776 us (1.48)
  blocking collectives: 0 us -> 564 us
  waiting for transfers between devices: 469 us -> 159 us
    all_to_all x0 -> x1, blocking collectives: none -> 564 us  [shards(): lax.all_to_all(jnp.stack([weighted] * lax.axis_size('phase')), 'phase', 0...]
    all_gather x1 -> x0, waiting for transfers between devices: 308 us -> none  [shards(): lax.all_gather(weighted, 'phase', axis=0, tiled=True)]
    unnamed x3 -> x2, waiting for transfers between devices: 148 us -> 146 us
  transfers between devices with their start and end apart: 3 -> 2, of which waited for: 3 -> 2; matrix products, arithmetic and copies ran while one was open for 0% -> 0% of each run, Pallas kernels for 0% -> 0%
where the time goes in v1:
time: 776 us
  blocking collectives  564 us (73%)
  waiting for transfers between devices  159 us (20%)
  matrix products  15.1 us (2%)
  between operations  13.5 us (2%)
  starting transfers between devices  12.9 us (2%)
  local copies, waits for them, and re-layouts  9.23 us (1%)
    all_to_all x1, blocking collectives, shards(): lax.all_to_all(jnp.stack([weighted] * lax.axis_size('phase')), 'phase', 0...  564 us
    unnamed x2, waiting for transfers between devices  146 us
  transfers between devices with their start and end apart: 2, of which 2 were waited for; matrix products, arithmetic and copies ran while one was open for 0% of the time, Pallas kernels for 0%

profile of v1, /device:TPU:2, one launch (start us, length us, event | category | flops | bytes accessed | tf_op | source)
XLA Modules:
  0.0 775.8 jit_solution(9211817756864416732)
XLA Ops:
  6.5 0.0 copy-start
  6.5 0.0 reduce-scatter.4.cloned.1.call-start
  6.5 1.3 broadcast_multiply_fusion
  7.9 1.6 stack.2
  9.5 563.7 %all_to_all.20 = f32[16,64,3072]{2,1,0:T(8,128)S(1)} all-to-all(f32[16,64,3072]{2,1,0:T(8,128)S(1)} %stack.2), channel_id=1, replica_groups=mesh['phase'=16,'slab'=32] {'phase'}, dimensions={0} | all-to-all | bytes 25165824 | tf_op jit(solution)/shard_map/all_to_all | solution.py:28
  573.2 0.0 copy-start.1
  573.2 0.0 copy-done
  573.2 11.2 %fusion.12 = f32[1024,256]{1,0:T(8,128)} fusion(f32[1024,3072]{1,0:T(8,128)S(1)} %bitcast.37, f32[256,3072]{1,0:T(8,128)S(1)} %bitcast.36), kind=kOutput, calls=%fused_computation.19 | convolution fusion | flops 9663676416 | bytes 16777216 | tf_op jit(solution)/shard_map/dot_general | solution.py:25
  584.4 2.5 copy.12
  587.0 0.0 copy-done.1
  587.0 2.9 convolution_bitcast_fusion
  589.9 2.5 copy.20
  592.4 0.0 reduce-scatter.4.cloned.1.call-update
  592.4 0.1 fusion.6
  592.6 145.7 %reduce-scatter.4.cloned.1.call-done = f32[32,256]{1,0:T(8,128)} async-done(((f32[1024,256]{1,0:T(8,128)}), f32[32,256]{1,0:T(8,128)}) %reduce-scatter.4.cloned.1.call-update) | async-done | bytes 32784
  738.2 0.9 copy.19
  739.1 0.1 copy.22
  739.2 0.8 reshape.45
  739.9 12.9 %all-to-all-start.1 = ((f32[16,1,512]{2,1,0:T(1,128)}), f32[16,1,512]{2,1,0:T(1,128)S(1)}, u32[]{:S(2)}, u32[]{:S(2)}) async-start(f32[16,1,512]{2,1,0:T(1,128)} %reshape.45), calls=%async_computation.1 | async-start | bytes 65536 | tf_op jit(solution)/shard_map/all_to_all | solution.py:47
  752.9 0.1 fusion.8
  753.0 0.1 maximum_multiply_fusion
  753.1 13.2 %all-to-all-done.1 = f32[16,1,512]{2,1,0:T(1,128)S(1)} async-done(((f32[16,1,512]{2,1,0:T(1,128)}), f32[16,1,512]{2,1,0:T(1,128)S(1)}, u32[]{:S(2)}, u32[]{:S(2)}) %all-to-all-start.1) | async-done | bytes 32800 | tf_op jit(solution)/shard_map/all_to_all | solution.py:47
  766.3 0.5 broadcast.26
  766.8 0.7 reduce
  767.6 0.1 reshape.46
  767.8 0.1 reshape.39
  767.9 0.1 copy.16
  768.0 1.0 fusion.13
  (2 shorter events, 0.1 us)
Async XLA Ops:
  6.5 566.7 %copy-start = (f32[2,4,32,3072]{3,2,1,0:T(8,128)S(1)}, f32[2,4,32,3072]{3,2,1,0:T(8,128)}, u32[]{:S(2)}) copy-start(f32[2,4,32,3072]{3,2,1,0:T(8,128)} %param.4) | copy-start | bytes 9437188
  6.5 731.7 %reduce-scatter.4.cloned.1.call-start = ((), (), s32[]{:S(2)}) async-start(), calls=%async_computation.3 | async-start | bytes 1081344
  573.2 13.8 %copy-start.1 = (s32[8]{0:T(128)S(1)}, s32[8]{0:T(128)}, u32[]{:S(2)}) copy-start(s32[8]{0:T(128)} %param.7) | copy-start | bytes 100
  739.9 26.4 %all-to-all-start.1 = ((f32[16,1,512]{2,1,0:T(1,128)}), f32[16,1,512]{2,1,0:T(1,128)S(1)}, u32[]{:S(2)}, u32[]{:S(2)}) async-start(f32[16,1,512]{2,1,0:T(1,128)} %reshape.45), calls=%async_computation.1 | async-start | bytes 65536 | tf_op jit(solution)/shard_map/all_to_all | solution.py:47
Sparse Core Ops, SparseCore 0:
  592.5 145.6 reduce-scatter.3
